TPU v7x, 256 devices: a whole 4x4x8 slice. The times are simulated.
256 devices in a mesh: ctx: 64 (over x_hi, z, y), head: 4 (over x_lo, core).
Axes of the slice: x: 4 (x_hi: 2, x_lo: 2; x = x_hi * 2 + x_lo), y: 4, z: 8, core: 2. Of those that a mesh axis runs over, the one named last changes fastest.
Arguments:
- queries: bfloat16 [8192, 16, 128], P('ctx', 'head'), may hold values from -30 to 30
- rotated_keys: bfloat16 [8192, 8, 128], P('ctx', 'head'), may hold values from -4 to 4
- value_vectors: bfloat16 [8192, 8, 128], P('ctx', 'head'), may hold values from -6 to 6
- out_grad: bfloat16 [8192, 5376], P('ctx', 'head'), may hold values from -16 to 16
- out_proj: bfloat16 [5376, 2048], P('ctx', 'head'), may hold values from -0.125 to 0.125
- seg_ids: int32 [8192], replicated, may hold values from 0 to 15, never falling along the last dimension, each value on 1 to 4096 neighbouring positions
Outputs:
- layer_out: bfloat16 [8192, 5376], P('ctx', 'head')
- query_gradient: bfloat16 [8192, 16, 128], P('ctx', 'head')
- grad_key: bfloat16 [8192, 8, 128], P('ctx', 'head')
- grad_value: bfloat16 [8192, 8, 128], P('ctx', 'head')
- grad_proj: float32 [5376, 2048], P('ctx', 'head')
Inputs may be any that keep to these rules, and one draw needn't show every extreme that they name: `seg_ids`: segment ids never fall along the slab; every one of the 16 books holds one token or more.
All inputs are finite; a program needn't handle non-finite values.
Results may differ from a plain program's by a relative error of at most 0.025.
Values may be sent and summed in bfloat16 or wider, within the bound.
No kernel may reach another device: no remote copies, remote signals or barrier semaphores. Data moves between devices by JAX's collectives and lax.ppermute only.
A program may use at most 128 MiB of HBM per device.

v0:
```python
import jax
import jax.numpy as jnp
from jax import lax
from jax.sharding import PartitionSpec as P

WINDOW_TOKENS = 1024


def passed_along(value, axis, by):
    count = lax.axis_size(axis)
    pairs = [(i, i + by) for i in range(count) if 0 <= i + by < count]
    return lax.ppermute(value, axis, pairs)


def shards(queries, rotated_keys, value_vectors, out_grad, out_proj, seg_ids):
    logit_scale = 168.0 ** (-0.5)
    tok_rows = queries.shape[0]
    heads_query = queries.shape[1]
    heads_kv = rotated_keys.shape[1]
    head_size = queries.shape[2]
    group_size = heads_query // heads_kv
    blocks = WINDOW_TOKENS // tok_rows
    ctx_count = lax.axis_size("ctx")
    ctx_index = lax.axis_index("ctx")
    own_block = jnp.stack([rotated_keys, value_vectors])
    received = []
    for offset in range(blocks):
        received.append(passed_along(own_block, "ctx", offset + 1))
    key_value = jnp.concatenate(received[::-1] + [own_block], axis=1)
    key_row_slice = key_value[0]
    value_row_slice = key_value[1]
    first_row = ctx_index * tok_rows
    seg_padded = jnp.concatenate([jnp.full((WINDOW_TOKENS,), -1, jnp.int32), seg_ids], 0)
    key_seg = lax.dynamic_slice_in_dim(seg_padded, first_row, WINDOW_TOKENS + tok_rows, 0)
    query_seg = lax.dynamic_slice_in_dim(seg_ids, first_row, tok_rows, 0)
    query_pos = first_row + jnp.arange(tok_rows, dtype=jnp.int32)
    key_pos = first_row - WINDOW_TOKENS + jnp.arange(WINDOW_TOKENS + tok_rows, dtype=jnp.int32)
    allowed = (key_pos[None, :] <= query_pos[:, None]) & (
        query_pos[:, None] - key_pos[None, :] < WINDOW_TOKENS
    )
    allowed = allowed & (key_pos[None, :] >= 0) & (query_seg[:, None] == key_seg[None, :])
    grouped_queries = queries.reshape(tok_rows, heads_kv, group_size, head_size)
    attention_logits = logit_scale * jnp.einsum(
        "eqco,fqo->qcef", grouped_queries, key_row_slice, preferred_element_type=jnp.float32
    )
    attention_logits = jnp.where(allowed, attention_logits, -1e30)
    top_score = jnp.max(attention_logits, axis=3, keepdims=True)
    weights = jnp.where(allowed, jnp.exp(attention_logits - top_score), 0.0)
    probs = weights / jnp.sum(weights, axis=3, keepdims=True)
    probabilities_half = probs.astype(jnp.bfloat16)
    attended_output = jnp.einsum(
        "ykip,pyj->iykj", probabilities_half, value_row_slice, preferred_element_type=jnp.float32
    )
    attended_output = attended_output.astype(jnp.bfloat16).reshape(
        tok_rows, heads_query * head_size
    )
    proj_full = lax.all_gather(out_proj, "ctx", axis=0, tiled=True)
    out_partial = lax.dot_general(
        attended_output, proj_full, (((1,), (1,)), ((), ())), preferred_element_type=jnp.float32
    )
    layer_out = lax.psum_scatter(out_partial, "head", scatter_dimension=1, tiled=True).astype(
        jnp.bfloat16
    )
    grad_full = lax.all_gather(out_grad, "head", axis=1, tiled=True)
    grad_attended = jnp.dot(grad_full, proj_full, preferred_element_type=jnp.float32).astype(
        jnp.bfloat16
    )
    proj_rows = grad_full.shape[1] // ctx_count
    proj_partial = jnp.einsum(
        "tcr,tj->crj",
        grad_full.reshape(tok_rows, ctx_count, proj_rows),
        attended_output,
        preferred_element_type=jnp.float32,
    )
    proj_summed = lax.psum_scatter(proj_partial, "ctx", scatter_dimension=0, tiled=True)
    grad_proj = proj_summed.reshape(proj_rows, -1) * (ctx_count * tok_rows) ** (-0.5)
    grouped_gradient = grad_attended.reshape(tok_rows, heads_kv, group_size, head_size)
    attn_groups = attended_output.reshape(tok_rows, heads_kv, group_size, head_size)
    probability_gradient = jnp.einsum(
        "eqco,fqo->qcef", grouped_gradient, value_row_slice, preferred_element_type=jnp.float32
    )
    row_delta = jnp.sum(
        grouped_gradient.astype(jnp.float32) * attn_groups.astype(jnp.float32), axis=3
    )
    row_delta = jnp.transpose(row_delta, (1, 2, 0))[..., None]
    score_gradient = (probs * (probability_gradient - row_delta)).astype(jnp.bfloat16)
    query_gradient = logit_scale * jnp.einsum(
        "ykip,pyj->iykj", score_gradient, key_row_slice, preferred_element_type=jnp.float32
    )
    query_gradient = query_gradient.astype(jnp.bfloat16).reshape(tok_rows, heads_query, head_size)
    key_portion = logit_scale * jnp.einsum(
        "huoe,ohul->ehl", score_gradient, grouped_queries, preferred_element_type=jnp.float32
    )
    value_portion = jnp.einsum(
        "huoe,ohul->ehl", probabilities_half, grouped_gradient, preferred_element_type=jnp.float32
    )
    both_parts = jnp.stack([key_portion, value_portion])
    halo_part = both_parts[:, :WINDOW_TOKENS]
    summed = both_parts[:, WINDOW_TOKENS:]
    for offset in range(blocks):
        distance = offset + 1
        portion = halo_part[:, (blocks - distance) * tok_rows : (blocks - distance + 1) * tok_rows]
        summed = summed + passed_along(portion, "ctx", -distance)
    grad_key = summed[0].astype(jnp.bfloat16)
    grad_value = summed[1].astype(jnp.bfloat16)
    return (layer_out, query_gradient, grad_key, grad_value, grad_proj)


def solution(mesh):
    return jax.shard_map(
        shards,
        mesh=mesh,
        in_specs=(
            P("ctx", "head", None),
            P("ctx", "head", None),
            P("ctx", "head", None),
            P("ctx", "head"),
            P("ctx", "head"),
            P(),
        ),
        out_specs=(
            P("ctx", "head"),
            P("ctx", "head", None),
            P("ctx", "head", None),
            P("ctx", "head", None),
            P("ctx", "head"),
        ),
        check_vma=False,
    )
```

profile of v0, /device:TPU:6, one launch (start us, length us, event | category | flops | bytes accessed | tf_op | source)
XLA Modules:
  0.0 658.0 jit_solution(7047656950511083596)
XLA Ops:
  8.9 3.5 collective-permute-start.7
  12.4 4.8 collective-permute-start.6
  17.2 4.6 collective-permute-start.5
  21.8 4.5 collective-permute-start.1
  26.3 5.5 collective-permute-start
  34.5 5.3 collective-permute-done
  39.7 8.6 %collective-permute-start.2 = (bf16[2,128,2,128]{3,1,2,0:T(8,128)(2,1)S(1)}, bf16[2,128,2,128]{3,1,2,0:T(8,128)(2,1)S(1)}, u32[]{:S(2)}, u32[]{:S(2)}) collective-permute-start(bf16[2,128,2,128]{3,1,2,0:T(8,128)(2,1)S(1)} %pad_maximum_fusion.1), channel_id=1, source_target_pairs={{0,24},{4,28},{8,32},{12,36},{16,40},{20,44},{24,48},{28,52},{32,5... | collective-permute-start | bytes 393224 | tf_op jit(solution)/shard_map/ppermute | solution.py:12
  50.3 4.2 collective-permute-done.2
  54.5 6.3 collective-permute-start.4
  60.8 3.0 collective-permute-done.3
  65.1 2.4 fusion.42
  69.4 79.3 %all-gather.6.cloned.1.call-done = bf16[64,84,512]{2,1,0:T(8,128)(2,1)} async-done(((bf16[1,84,512]{2,1,0:T(8,128)(2,1)}), bf16[64,84,512]{2,1,0:T(8,128)(2,1)}) %all-gather.6.cloned.1.call-update) | async-done | bytes 5505040 | tf_op jit(solution)/shard_map/all_gather | solution.py:57
  148.7 8.9 %reshape.53 = bf16[5376,512]{1,0:T(8,128)(2,1)} reshape(bf16[64,84,512]{2,1,0:T(8,128)(2,1)} %all-gather.6.cloned.1.call-done) | data formatting | bytes 11010048
  157.6 16.0 %all-gather.4.cloned.1.call-done = bf16[128,5376]{0,1:T(8,128)(2,1)} async-done(((bf16[128,1344]{0,1:T(8,128)(2,1)}), bf16[128,5376]{0,1:T(8,128)(2,1)}) %all-gather.4.cloned.1.call-update) | async-done | bytes 1376272 | tf_op jit(solution)/shard_map/all_gather | solution.py:64
  173.6 3.9 convolution_convert_fusion
  178.0 5.8 fusion.45
  183.9 2.2 reshape.51
  186.1 6.0 convolution_bitcast_fusion
  193.4 2.1 fusion.8
  197.8 8.3 %collective-permute-start.8 = (f32[2,128,2,128]{3,1,2,0:T(8,128)S(1)}, f32[2,128,2,128]{3,1,2,0:T(8,128)S(1)}, u32[]{:S(2)}, u32[]{:S(2)}) collective-permute-start(f32[2,128,2,128]{3,1,2,0:T(8,128)S(1)} %get-tuple-element.20), channel_id=1, source_target_pairs={{4,0},{8,4},{12,8},{16,12},{20,16},{24,20},{28,24},{32,28},{36,32}... | collective-permute-start | bytes 786440 | tf_op jit(solution)/shard_map/ppermute | solution.py:12
  206.1 2.7 collective-permute-start.9
  208.9 3.6 collective-permute-start.10
  212.5 3.3 collective-permute-start.11
  215.8 5.1 collective-permute-start.12
  220.9 3.2 collective-permute-start.13
  224.1 3.3 collective-permute-start.15
  227.5 5.3 collective-permute-start.14
  234.0 9.8 %collective-permute-done.12 = f32[2,128,2,128]{3,1,2,0:T(8,128)} collective-permute-done((f32[2,128,2,128]{3,1,2,0:T(8,128)}, f32[2,128,2,128]{3,1,2,0:T(8,128)}, u32[]{:S(2)}, u32[]{:S(2)}) %collective-permute-start.12) | collective-permute-done | bytes 262176 | tf_op jit(solution)/shard_map/ppermute | solution.py:12
  243.8 10.8 %collective-permute-done.13 = f32[2,128,2,128]{3,1,2,0:T(8,128)} collective-permute-done((f32[2,128,2,128]{3,1,2,0:T(8,128)}, f32[2,128,2,128]{3,1,2,0:T(8,128)}, u32[]{:S(2)}, u32[]{:S(2)}) %collective-permute-start.13) | collective-permute-done | bytes 262176 | tf_op jit(solution)/shard_map/ppermute | solution.py:12
  254.6 12.0 %collective-permute-done.15 = f32[2,128,2,128]{3,1,2,0:T(8,128)} collective-permute-done((f32[2,128,2,128]{3,1,2,0:T(8,128)}, f32[2,128,2,128]{3,1,2,0:T(8,128)}, u32[]{:S(2)}, u32[]{:S(2)}) %collective-permute-start.15) | collective-permute-done | bytes 262176 | tf_op jit(solution)/shard_map/ppermute | solution.py:12
  266.6 11.9 %collective-permute-done.14 = f32[2,128,2,128]{3,1,2,0:T(8,128)} collective-permute-done((f32[2,128,2,128]{3,1,2,0:T(8,128)S(1)}, f32[2,128,2,128]{3,1,2,0:T(8,128)}, u32[]{:S(2)}, u32[]{:S(2)}) %collective-permute-start.14) | collective-permute-done | bytes 262176 | tf_op jit(solution)/shard_map/ppermute | solution.py:12
  283.3 366.5 %reduce-scatter.5.cloned.1.call-done = f32[1,84,512]{2,1,0:T(8,128)} async-done(((f32[64,84,512]{2,1,0:T(8,128)}), f32[1,84,512]{2,1,0:T(8,128)}) %reduce-scatter.5.cloned.1.call-update) | async-done | bytes 172048 | tf_op jit(solution)/shard_map/reduce_scatter | solution.py:75
  (63 shorter events, 21.1 us)
Async XLA Ops:
  7.2 57.9 %copy-start = (bf16[128,4,128]{2,1,0:T(4,128)(2,1)S(1)}, bf16[128,4,128]{2,1,0:T(4,128)(2,1)}, u32[]{:S(2)}) copy-start(bf16[128,4,128]{2,1,0:T(4,128)(2,1)} %param.6) | copy-start | bytes 393220
  7.2 141.5 %all-gather.6.cloned.1.call-start = ((), (), s32[]{:S(2)}) async-start(), calls=%async_computation.5 | async-start | bytes 5857280 | tf_op jit(solution)/shard_map/all_gather | solution.py:57
  7.9 165.7 %all-gather.4.cloned.1.call-start = ((), (), s32[]{:S(2)}) async-start(), calls=%async_computation.3 | async-start | bytes 1720320 | tf_op jit(solution)/shard_map/all_gather | solution.py:64
  8.9 56.1 %collective-permute-start.7 = (bf16[2,128,2,128]{3,1,2,0:T(8,128)(2,1)S(1)}, bf16[2,128,2,128]{3,1,2,0:T(8,128)(2,1)S(1)}, u32[]{:S(2)}, u32[]{:S(2)}) collective-permute-start(bf16[2,128,2,128]{3,1,2,0:T(8,128)(2,1)S(1)} %pad_maximum_fusion.1), channel_id=1, source_target_pairs={{0,4},{4,8},{8,12},{12,16},{16,20},{20,24},{24,28},{28,32},{32,36}... | collective-permute-start | bytes 393224 | tf_op jit(solution)/shard_map/ppermute | solution.py:12
  12.4 52.6 %collective-permute-start.6 = (bf16[2,128,2,128]{3,1,2,0:T(8,128)(2,1)S(1)}, bf16[2,128,2,128]{3,1,2,0:T(8,128)(2,1)S(1)}, u32[]{:S(2)}, u32[]{:S(2)}) collective-permute-start(bf16[2,128,2,128]{3,1,2,0:T(8,128)(2,1)S(1)} %pad_maximum_fusion.1), channel_id=1, source_target_pairs={{0,8},{4,12},{8,16},{12,20},{16,24},{20,28},{24,32},{28,36},{32,40... | collective-permute-start | bytes 393224 | tf_op jit(solution)/shard_map/ppermute | solution.py:12
  17.2 47.8 %collective-permute-start.5 = (bf16[2,128,2,128]{3,1,2,0:T(8,128)(2,1)S(1)}, bf16[2,128,2,128]{3,1,2,0:T(8,128)(2,1)S(1)}, u32[]{:S(2)}, u32[]{:S(2)}) collective-permute-start(bf16[2,128,2,128]{3,1,2,0:T(8,128)(2,1)S(1)} %pad_maximum_fusion.1), channel_id=1, source_target_pairs={{0,12},{4,16},{8,20},{12,24},{16,28},{20,32},{24,36},{28,40},{32,4... | collective-permute-start | bytes 393224 | tf_op jit(solution)/shard_map/ppermute | solution.py:12
  21.8 26.5 %collective-permute-start.1 = (bf16[2,128,2,128]{3,1,2,0:T(8,128)(2,1)S(1)}, bf16[2,128,2,128]{3,1,2,0:T(8,128)(2,1)S(1)}, u32[]{:S(2)}, u32[]{:S(2)}) collective-permute-start(bf16[2,128,2,128]{3,1,2,0:T(8,128)(2,1)S(1)} %pad_maximum_fusion.1), channel_id=1, source_target_pairs={{0,28},{4,32},{8,36},{12,40},{16,44},{20,48},{24,52},{28,56},{32,6... | collective-permute-start | bytes 393224 | tf_op jit(solution)/shard_map/ppermute | solution.py:12
  26.3 13.5 %collective-permute-start = (bf16[2,128,2,128]{3,1,2,0:T(8,128)(2,1)S(1)}, bf16[2,128,2,128]{3,1,2,0:T(8,128)(2,1)S(1)}, u32[]{:S(2)}, u32[]{:S(2)}) collective-permute-start(bf16[2,128,2,128]{3,1,2,0:T(8,128)(2,1)S(1)} %pad_maximum_fusion.1), channel_id=1, source_target_pairs={{0,32},{4,36},{8,40},{12,44},{16,48},{20,52},{24,56},{28,60},{32,6... | collective-permute-start | bytes 393224 | tf_op jit(solution)/shard_map/ppermute | solution.py:12
  31.8 249.6 %reduce-scatter.3.cloned.1.call-start = ((), (), s32[]{:S(2)}) async-start(), calls=%async_computation.2 | async-start | bytes 3440640 | tf_op jit(solution)/shard_map/reduce_scatter | solution.py:61
  39.7 14.7 %collective-permute-start.2 = (bf16[2,128,2,128]{3,1,2,0:T(8,128)(2,1)S(1)}, bf16[2,128,2,128]{3,1,2,0:T(8,128)(2,1)S(1)}, u32[]{:S(2)}, u32[]{:S(2)}) collective-permute-start(bf16[2,128,2,128]{3,1,2,0:T(8,128)(2,1)S(1)} %pad_maximum_fusion.1), channel_id=1, source_target_pairs={{0,24},{4,28},{8,32},{12,36},{16,40},{20,44},{24,48},{28,52},{32,5... | collective-permute-start | bytes 393224 | tf_op jit(solution)/shard_map/ppermute | solution.py:12
  48.3 15.4 %collective-permute-start.3 = (bf16[2,128,2,128]{3,1,2,0:T(8,128)(2,1)S(1)}, bf16[2,128,2,128]{3,1,2,0:T(8,128)(2,1)S(1)}, u32[]{:S(2)}, u32[]{:S(2)}) collective-permute-start(bf16[2,128,2,128]{3,1,2,0:T(8,128)(2,1)S(1)} %pad_maximum_fusion.1), channel_id=1, source_target_pairs={{0,20},{4,24},{8,28},{12,32},{16,36},{20,40},{24,44},{28,48},{32,5... | collective-permute-start | bytes 393224 | tf_op jit(solution)/shard_map/ppermute | solution.py:12
  54.5 10.5 %collective-permute-start.4 = (bf16[2,128,2,128]{3,1,2,0:T(8,128)(2,1)S(1)}, bf16[2,128,2,128]{3,1,2,0:T(8,128)(2,1)S(1)}, u32[]{:S(2)}, u32[]{:S(2)}) collective-permute-start(bf16[2,128,2,128]{3,1,2,0:T(8,128)(2,1)S(1)} %pad_maximum_fusion.1), channel_id=1, source_target_pairs={{0,16},{4,20},{8,24},{12,28},{16,32},{20,36},{24,40},{28,44},{32,4... | collective-permute-start | bytes 393224 | tf_op jit(solution)/shard_map/ppermute | solution.py:12
  65.1 112.5 %copy-start.3 = (bf16[2,1152,2,128]{3,1,2,0:T(8,128)(2,1)}, bf16[2,1152,2,128]{3,1,2,0:T(8,128)(2,1)S(1)}, u32[]{:S(2)}) copy-start(bf16[2,1152,2,128]{3,1,2,0:T(8,128)(2,1)S(1)} %constant_dynamic-update-slice_fusion) | copy-start | bytes 3538948
  183.8 466.0 %reduce-scatter.5.cloned.1.call-start = ((), (), s32[]{:S(2)}) async-start(), calls=%async_computation.4 | async-start | bytes 11714560 | tf_op jit(solution)/shard_map/reduce_scatter | solution.py:75
  192.1 1.3 copy-start.4
  196.5 1.4 copy-start.1
  196.5 36.4 %copy-start.5 = (bf16[2,1152,2,128]{3,1,2,0:T(8,128)(2,1)S(1)}, bf16[2,1152,2,128]{3,1,2,0:T(8,128)(2,1)}, u32[]{:S(2)}) copy-start(bf16[2,1152,2,128]{3,1,2,0:T(8,128)(2,1)} %copy-done.3) | copy-start | bytes 3538948
  197.8 80.7 %copy-start.2 = (f32[1,1152,2,128]{3,1,2,0:T(8,128)S(1)}, f32[1,1152,2,128]{3,1,2,0:T(8,128)}, u32[]{:S(2)}) copy-start(f32[1,1152,2,128]{3,1,2,0:T(8,128)} %copy-done.1) | copy-start | bytes 3538948
  197.8 23.0 %collective-permute-start.8 = (f32[2,128,2,128]{3,1,2,0:T(8,128)S(1)}, f32[2,128,2,128]{3,1,2,0:T(8,128)S(1)}, u32[]{:S(2)}, u32[]{:S(2)}) collective-permute-start(f32[2,128,2,128]{3,1,2,0:T(8,128)S(1)} %get-tuple-element.20), channel_id=1, source_target_pairs={{4,0},{8,4},{12,8},{16,12},{20,16},{24,20},{28,24},{32,28},{36,32}... | collective-permute-start | bytes 786440 | tf_op jit(solution)/shard_map/ppermute | solution.py:12
  206.1 18.0 %collective-permute-start.9 = (f32[2,128,2,128]{3,1,2,0:T(8,128)S(1)}, f32[2,128,2,128]{3,1,2,0:T(8,128)S(1)}, u32[]{:S(2)}, u32[]{:S(2)}) collective-permute-start(f32[2,128,2,128]{3,1,2,0:T(8,128)S(1)} %get-tuple-element.21), channel_id=1, source_target_pairs={{8,0},{12,4},{16,8},{20,12},{24,16},{28,20},{32,24},{36,28},{40,32... | collective-permute-start | bytes 786440 | tf_op jit(solution)/shard_map/ppermute | solution.py:12
  208.9 18.6 %collective-permute-start.10 = (f32[2,128,2,128]{3,1,2,0:T(8,128)S(1)}, f32[2,128,2,128]{3,1,2,0:T(8,128)S(1)}, u32[]{:S(2)}, u32[]{:S(2)}) collective-permute-start(f32[2,128,2,128]{3,1,2,0:T(8,128)S(1)} %get-tuple-element.22), channel_id=1, source_target_pairs={{12,0},{16,4},{20,8},{24,12},{28,16},{32,20},{36,24},{40,28},{44,3... | collective-permute-start | bytes 786440 | tf_op jit(solution)/shard_map/ppermute | solution.py:12
  212.5 21.5 %collective-permute-start.11 = (f32[2,128,2,128]{3,1,2,0:T(8,128)}, f32[2,128,2,128]{3,1,2,0:T(8,128)}, u32[]{:S(2)}, u32[]{:S(2)}) collective-permute-start(f32[2,128,2,128]{3,1,2,0:T(8,128)} %get-tuple-element.23), channel_id=1, source_target_pairs={{16,0},{20,4},{24,8},{28,12},{32,16},{36,20},{40,24},{44,28},{48,3... | collective-permute-start | bytes 786440 | tf_op jit(solution)/shard_map/ppermute | solution.py:12
  215.8 28.0 %collective-permute-start.12 = (f32[2,128,2,128]{3,1,2,0:T(8,128)}, f32[2,128,2,128]{3,1,2,0:T(8,128)}, u32[]{:S(2)}, u32[]{:S(2)}) collective-permute-start(f32[2,128,2,128]{3,1,2,0:T(8,128)} %get-tuple-element.24), channel_id=1, source_target_pairs={{20,0},{24,4},{28,8},{32,12},{36,16},{40,20},{44,24},{48,28},{52,3... | collective-permute-start | bytes 786440 | tf_op jit(solution)/shard_map/ppermute | solution.py:12
  220.9 33.8 %collective-permute-start.13 = (f32[2,128,2,128]{3,1,2,0:T(8,128)}, f32[2,128,2,128]{3,1,2,0:T(8,128)}, u32[]{:S(2)}, u32[]{:S(2)}) collective-permute-start(f32[2,128,2,128]{3,1,2,0:T(8,128)} %get-tuple-element.25), channel_id=1, source_target_pairs={{24,0},{28,4},{32,8},{36,12},{40,16},{44,20},{48,24},{52,28},{56,3... | collective-permute-start | bytes 786440 | tf_op jit(solution)/shard_map/ppermute | solution.py:12
  224.1 42.5 %collective-permute-start.15 = (f32[2,128,2,128]{3,1,2,0:T(8,128)}, f32[2,128,2,128]{3,1,2,0:T(8,128)}, u32[]{:S(2)}, u32[]{:S(2)}) collective-permute-start(f32[2,128,2,128]{3,1,2,0:T(8,128)} %get-tuple-element.26), channel_id=1, source_target_pairs={{32,0},{36,4},{40,8},{44,12},{48,16},{52,20},{56,24},{60,28},{64,3... | collective-permute-start | bytes 786440 | tf_op jit(solution)/shard_map/ppermute | solution.py:12
  227.5 5.8 copy-start.6
  227.5 51.1 %collective-permute-start.14 = (f32[2,128,2,128]{3,1,2,0:T(8,128)S(1)}, f32[2,128,2,128]{3,1,2,0:T(8,128)}, u32[]{:S(2)}, u32[]{:S(2)}) collective-permute-start(f32[2,128,2,128]{3,1,2,0:T(8,128)S(1)} %get-tuple-element.27), channel_id=1, source_target_pairs={{28,0},{32,4},{36,8},{40,12},{44,16},{48,20},{52,24},{56,28},{60,3... | collective-permute-start | bytes 786440 | tf_op jit(solution)/shard_map/ppermute | solution.py:12
Sparse Core Ops, SparseCore 0:
  11.6 137.0 all-gather.5
  150.5 23.0 all-gather.3
  183.9 37.0 reduce-scatter.2
  223.5 426.2 reduce-scatter.4
where the time goes:
time: 659 us; the launch traced here: 658 us
  waiting for transfers between devices  521 us (79%)
  starting transfers between devices  74.7 us (11%)
  matrix products  22 us (3%)
  local copies, waits for them, and re-layouts  16.8 us (3%)
  between operations  14.2 us (2%)
  other arithmetic  9.75 us (1%)
    reduce_scatter x1, waiting for transfers between devices, shards(): lax.psum_scatter(proj_partial, 'ctx', scatter_dimension=0, tiled=True)  367 us
    all_gather x1, waiting for transfers between devices, shards(): proj_full = lax.all_gather(out_proj, 'ctx', axis=0, tiled=True)  79.3 us
    ppermute x16, starting transfers between devices, passed_along(): return lax.ppermute(value, axis, pairs)  74.5 us
    ppermute x16, waiting for transfers between devices, passed_along(): return lax.ppermute(value, axis, pairs)  58.1 us
    all_gather x1, waiting for transfers between devices, shards(): grad_full = lax.all_gather(out_grad, 'head', axis=1, tiled=True)  16 us
  transfers between devices with their start and end apart: 20, of which 11 were waited for; matrix products, arithmetic and copies ran while one was open for 5% of the time, Pallas kernels for 0%

commit v1 on v0

--- a/solution.py
+++ b/solution.py
@@ -61,7 +61,12 @@
     layer_out = lax.psum_scatter(out_partial, "head", scatter_dimension=1, tiled=True).astype(
         jnp.bfloat16
     )
-    grad_full = lax.all_gather(out_grad, "head", axis=1, tiled=True)
+    grad_full = jnp.concatenate(
+        lax.all_to_all(
+            jnp.stack(tuple((out_grad for _ in range(lax.axis_size("head")))), axis=0), "head", 0, 0
+        ),
+        1,
+    )
     grad_attended = jnp.dot(grad_full, proj_full, preferred_element_type=jnp.float32).astype(
         jnp.bfloat16
     )

time: 659 us -> 648 us (0.983)
  waiting for transfers between devices: 521 us -> 503 us
    all_gather x1 -> x0, waiting for transfers between devices: 16 us -> none  [shards(): grad_full = lax.all_gather(out_grad, 'head', axis=1, tiled=True)]
    ppermute x16, waiting for transfers between devices: 58.1 us -> 46.1 us  [passed_along(): return lax.ppermute(value, axis, pairs)]
    reduce_scatter x1, waiting for transfers between devices: 367 us -> 377 us  [shards(): lax.psum_scatter(proj_partial, 'ctx', scatter_dimension=0, tiled=True)]
    unnamed x26 -> x30, local copies, waits for them, and re-layouts: 12.7 us -> 15.5 us
  transfers between devices with their start and end apart: 20 -> 20, of which waited for: 11 -> 9; matrix products, arithmetic and copies ran while one was open for 5% -> 6% of each run, Pallas kernels for 0% -> 0%
where the time goes in v1:
time: 648 us; the launch traced here: 646 us
  waiting for transfers between devices  503 us (78%)
  starting transfers between devices  75.7 us (12%)
  matrix products  24 us (4%)
  local copies, waits for them, and re-layouts  20.1 us (3%)
  between operations  14.2 us (2%)
  other arithmetic  9.06 us (1%)
    reduce_scatter x1, waiting for transfers between devices, shards(): lax.psum_scatter(proj_partial, 'ctx', scatter_dimension=0, tiled=True)  377 us
    all_gather x1, waiting for transfers between devices, shards(): proj_full = lax.all_gather(out_proj, 'ctx', axis=0, tiled=True)  78.7 us
    ppermute x16, starting transfers between devices, passed_along(): return lax.ppermute(value, axis, pairs)  71.2 us
    ppermute x16, waiting for transfers between devices, passed_along(): return lax.ppermute(value, axis, pairs)  46.1 us
    unnamed x30, local copies, waits for them, and re-layouts  15.5 us
  transfers between devices with their start and end apart: 20, of which 9 were waited for; matrix products, arithmetic and copies ran while one was open for 6% of the time, Pallas kernels for 0%

profile of v1, /device:TPU:6, one launch (start us, length us, event | category | flops | bytes accessed | tf_op | source)
XLA Modules:
  0.0 645.9 jit_solution(14024646602604563679)
XLA Ops:
  8.8 3.5 collective-permute-start.7
  12.3 4.8 collective-permute-start.6
  17.1 4.6 collective-permute-start.5
  21.8 4.5 collective-permute-start.1
  26.2 5.5 collective-permute-start
  31.7 2.3 stack.28
  34.0 4.5 all-to-all-start
  40.4 8.5 %collective-permute-start.2 = (bf16[2,128,2,128]{3,1,2,0:T(8,128)(2,1)S(1)}, bf16[2,128,2,128]{3,1,2,0:T(8,128)(2,1)S(1)}, u32[]{:S(2)}, u32[]{:S(2)}) collective-permute-start(bf16[2,128,2,128]{3,1,2,0:T(8,128)(2,1)S(1)} %pad_maximum_fusion.1), channel_id=1, source_target_pairs={{0,24},{4,28},{8,32},{12,36},{16,40},{20,44},{24,48},{28,52},{32,5... | collective-permute-start | bytes 393224 | tf_op jit(solution)/shard_map/ppermute | solution.py:12
  52.7 2.9 collective-permute-done.2
  55.6 6.9 %collective-permute-start.4 = (bf16[2,128,2,128]{3,1,2,0:T(8,128)(2,1)S(1)}, bf16[2,128,2,128]{3,1,2,0:T(8,128)(2,1)S(1)}, u32[]{:S(2)}, u32[]{:S(2)}) collective-permute-start(bf16[2,128,2,128]{3,1,2,0:T(8,128)(2,1)S(1)} %pad_maximum_fusion.1), channel_id=1, source_target_pairs={{0,16},{4,20},{8,24},{12,28},{16,32},{20,36},{24,40},{28,44},{32,4... | collective-permute-start | bytes 393224 | tf_op jit(solution)/shard_map/ppermute | solution.py:12
  62.5 4.1 collective-permute-done.3
  66.8 2.4 fusion.42
  71.1 78.7 %all-gather.3.cloned.1.call-done = bf16[64,84,512]{2,1,0:T(8,128)(2,1)} async-done(((bf16[1,84,512]{2,1,0:T(8,128)(2,1)}), bf16[64,84,512]{2,1,0:T(8,128)(2,1)}) %all-gather.3.cloned.1.call-update) | async-done | bytes 5505040 | tf_op jit(solution)/shard_map/all_gather | solution.py:57
  149.8 8.9 %reshape.59 = bf16[5376,512]{1,0:T(8,128)(2,1)} reshape(bf16[64,84,512]{2,1,0:T(8,128)(2,1)} %all-gather.3.cloned.1.call-done) | data formatting | bytes 11010048
  158.7 3.5 convolution_convert_fusion
  163.7 5.8 fusion.45
  170.8 7.4 %convolution_bitcast_fusion = f32[64,84,512]{2,1,0:T(8,128)} fusion(bf16[128,512,1]{0,1,2:T(8,128)(2,1)S(1)} %bitcast.113, bf16[128,64,84]{0,2,1:T(8,128)(2,1)} %reshape_reshape.3), kind=kOutput, calls=%fused_computation.17 | convolution fusion | flops 704643072 | bytes 12517376 | tf_op jit(solution)/shard_map/tcr,tj->crj/dot_general | solution.py:74
  179.7 2.1 fusion.8
  184.2 7.5 %collective-permute-start.8 = (f32[2,128,2,128]{3,1,2,0:T(8,128)S(1)}, f32[2,128,2,128]{3,1,2,0:T(8,128)S(1)}, u32[]{:S(2)}, u32[]{:S(2)}) collective-permute-start(f32[2,128,2,128]{3,1,2,0:T(8,128)S(1)} %get-tuple-element.20), channel_id=1, source_target_pairs={{4,0},{8,4},{12,8},{16,12},{20,16},{24,20},{28,24},{32,28},{36,32}... | collective-permute-start | bytes 786440 | tf_op jit(solution)/shard_map/ppermute | solution.py:12
  191.7 2.7 collective-permute-start.9
  194.4 3.0 collective-permute-start.10
  197.5 3.2 collective-permute-start.11
  200.7 4.1 collective-permute-start.12
  204.8 5.0 collective-permute-start.13
  209.8 3.6 collective-permute-start.15
  213.4 1.9 collective-permute-start.14
  216.5 21.2 %collective-permute-done.11 = f32[2,128,2,128]{3,1,2,0:T(8,128)} collective-permute-done((f32[2,128,2,128]{3,1,2,0:T(8,128)}, f32[2,128,2,128]{3,1,2,0:T(8,128)}, u32[]{:S(2)}, u32[]{:S(2)}) %collective-permute-start.11) | collective-permute-done | bytes 262176 | tf_op jit(solution)/shard_map/ppermute | solution.py:12
  237.7 5.8 collective-permute-done.12
  243.4 5.6 collective-permute-done.13
  249.1 3.8 collective-permute-done.15
  252.8 2.7 collective-permute-done.14
  260.3 377.5 %reduce-scatter.5.cloned.1.call-done = f32[1,84,512]{2,1,0:T(8,128)} async-done(((f32[64,84,512]{2,1,0:T(8,128)}), f32[1,84,512]{2,1,0:T(8,128)}) %reduce-scatter.5.cloned.1.call-update) | async-done | bytes 172048 | tf_op jit(solution)/shard_map/reduce_scatter | solution.py:80
  (67 shorter events, 23.5 us)
Async XLA Ops:
  7.2 59.6 %copy-start = (bf16[128,4,128]{2,1,0:T(4,128)(2,1)S(1)}, bf16[128,4,128]{2,1,0:T(4,128)(2,1)}, u32[]{:S(2)}) copy-start(bf16[128,4,128]{2,1,0:T(4,128)(2,1)} %param.6) | copy-start | bytes 393220
  7.2 142.6 %all-gather.3.cloned.1.call-start = ((), (), s32[]{:S(2)}) async-start(), calls=%async_computation.5 | async-start | bytes 5857280 | tf_op jit(solution)/shard_map/all_gather | solution.py:57
  8.8 57.9 %collective-permute-start.7 = (bf16[2,128,2,128]{3,1,2,0:T(8,128)(2,1)S(1)}, bf16[2,128,2,128]{3,1,2,0:T(8,128)(2,1)S(1)}, u32[]{:S(2)}, u32[]{:S(2)}) collective-permute-start(bf16[2,128,2,128]{3,1,2,0:T(8,128)(2,1)S(1)} %pad_maximum_fusion.1), channel_id=1, source_target_pairs={{0,4},{4,8},{8,12},{12,16},{16,20},{20,24},{24,28},{28,32},{32,36}... | collective-permute-start | bytes 393224 | tf_op jit(solution)/shard_map/ppermute | solution.py:12
  12.3 54.4 %collective-permute-start.6 = (bf16[2,128,2,128]{3,1,2,0:T(8,128)(2,1)S(1)}, bf16[2,128,2,128]{3,1,2,0:T(8,128)(2,1)S(1)}, u32[]{:S(2)}, u32[]{:S(2)}) collective-permute-start(bf16[2,128,2,128]{3,1,2,0:T(8,128)(2,1)S(1)} %pad_maximum_fusion.1), channel_id=1, source_target_pairs={{0,8},{4,12},{8,16},{12,20},{16,24},{20,28},{24,32},{28,36},{32,40... | collective-permute-start | bytes 393224 | tf_op jit(solution)/shard_map/ppermute | solution.py:12
  17.1 49.5 %collective-permute-start.5 = (bf16[2,128,2,128]{3,1,2,0:T(8,128)(2,1)S(1)}, bf16[2,128,2,128]{3,1,2,0:T(8,128)(2,1)S(1)}, u32[]{:S(2)}, u32[]{:S(2)}) collective-permute-start(bf16[2,128,2,128]{3,1,2,0:T(8,128)(2,1)S(1)} %pad_maximum_fusion.1), channel_id=1, source_target_pairs={{0,12},{4,16},{8,20},{12,24},{16,28},{20,32},{24,36},{28,40},{32,4... | collective-permute-start | bytes 393224 | tf_op jit(solution)/shard_map/ppermute | solution.py:12
  21.8 28.1 %collective-permute-start.1 = (bf16[2,128,2,128]{3,1,2,0:T(8,128)(2,1)S(1)}, bf16[2,128,2,128]{3,1,2,0:T(8,128)(2,1)}, u32[]{:S(2)}, u32[]{:S(2)}) collective-permute-start(bf16[2,128,2,128]{3,1,2,0:T(8,128)(2,1)S(1)} %pad_maximum_fusion.1), channel_id=1, source_target_pairs={{0,28},{4,32},{8,36},{12,40},{16,44},{20,48},{24,52},{28,56},{32,6... | collective-permute-start | bytes 393224 | tf_op jit(solution)/shard_map/ppermute | solution.py:12
  26.2 13.5 %collective-permute-start = (bf16[2,128,2,128]{3,1,2,0:T(8,128)(2,1)S(1)}, bf16[2,128,2,128]{3,1,2,0:T(8,128)(2,1)S(1)}, u32[]{:S(2)}, u32[]{:S(2)}) collective-permute-start(bf16[2,128,2,128]{3,1,2,0:T(8,128)(2,1)S(1)} %pad_maximum_fusion.1), channel_id=1, source_target_pairs={{0,32},{4,36},{8,40},{12,44},{16,48},{20,52},{24,56},{28,60},{32,6... | collective-permute-start | bytes 393224 | tf_op jit(solution)/shard_map/ppermute | solution.py:12
  34.0 4.5 copy-start.8
  34.0 124.7 %all-to-all-start = ((bf16[4,128,1344]{1,2,0:T(8,128)(2,1)}), bf16[4,128,1344]{1,2,0:T(8,128)(2,1)S(1)}, u32[]{:S(2)}, u32[]{:S(2)}) async-start(bf16[4,128,1344]{1,2,0:T(8,128)(2,1)} %stack.28), calls=%async_computation.1 | async-start | bytes 2752512 | tf_op jit(solution)/shard_map/all_to_all | solution.py:65
  38.5 219.9 %reduce-scatter.3.cloned.1.call-start = ((), (), s32[]{:S(2)}) async-start(), calls=%async_computation.3 | async-start | bytes 3440640 | tf_op jit(solution)/shard_map/reduce_scatter | solution.py:61
  39.7 0.7 copy-start.7
  40.4 15.2 %collective-permute-start.2 = (bf16[2,128,2,128]{3,1,2,0:T(8,128)(2,1)S(1)}, bf16[2,128,2,128]{3,1,2,0:T(8,128)(2,1)S(1)}, u32[]{:S(2)}, u32[]{:S(2)}) collective-permute-start(bf16[2,128,2,128]{3,1,2,0:T(8,128)(2,1)S(1)} %pad_maximum_fusion.1), channel_id=1, source_target_pairs={{0,24},{4,28},{8,32},{12,36},{16,40},{20,44},{24,48},{28,52},{32,5... | collective-permute-start | bytes 393224 | tf_op jit(solution)/shard_map/ppermute | solution.py:12
  49.8 16.8 %collective-permute-start.3 = (bf16[2,128,2,128]{3,1,2,0:T(8,128)(2,1)S(1)}, bf16[2,128,2,128]{3,1,2,0:T(8,128)(2,1)S(1)}, u32[]{:S(2)}, u32[]{:S(2)}) collective-permute-start(bf16[2,128,2,128]{3,1,2,0:T(8,128)(2,1)S(1)} %pad_maximum_fusion.1), channel_id=1, source_target_pairs={{0,20},{4,24},{8,28},{12,32},{16,36},{20,40},{24,44},{28,48},{32,5... | collective-permute-start | bytes 393224 | tf_op jit(solution)/shard_map/ppermute | solution.py:12
  55.6 11.0 %collective-permute-start.4 = (bf16[2,128,2,128]{3,1,2,0:T(8,128)(2,1)S(1)}, bf16[2,128,2,128]{3,1,2,0:T(8,128)(2,1)S(1)}, u32[]{:S(2)}, u32[]{:S(2)}) collective-permute-start(bf16[2,128,2,128]{3,1,2,0:T(8,128)(2,1)S(1)} %pad_maximum_fusion.1), channel_id=1, source_target_pairs={{0,16},{4,20},{8,24},{12,28},{16,32},{20,36},{24,40},{28,44},{32,4... | collective-permute-start | bytes 393224 | tf_op jit(solution)/shard_map/ppermute | solution.py:12
  66.8 2.5 copy-start.3
  169.5 468.3 %reduce-scatter.5.cloned.1.call-start = ((), (), s32[]{:S(2)}) async-start(), calls=%async_computation.4 | async-start | bytes 11714560 | tf_op jit(solution)/shard_map/reduce_scatter | solution.py:80
  178.2 1.5 copy-start.4
  182.8 1.4 copy-start.1
  182.8 32.5 %copy-start.5 = (bf16[2,1152,2,128]{3,1,2,0:T(8,128)(2,1)S(1)}, bf16[2,1152,2,128]{3,1,2,0:T(8,128)(2,1)}, u32[]{:S(2)}) copy-start(bf16[2,1152,2,128]{3,1,2,0:T(8,128)(2,1)} %copy-done.3) | copy-start | bytes 3538948
  184.2 71.4 %copy-start.2 = (f32[1,1152,2,128]{3,1,2,0:T(8,128)S(1)}, f32[1,1152,2,128]{3,1,2,0:T(8,128)}, u32[]{:S(2)}) copy-start(f32[1,1152,2,128]{3,1,2,0:T(8,128)} %copy-done.1) | copy-start | bytes 3538948
  184.2 20.6 %collective-permute-start.8 = (f32[2,128,2,128]{3,1,2,0:T(8,128)S(1)}, f32[2,128,2,128]{3,1,2,0:T(8,128)S(1)}, u32[]{:S(2)}, u32[]{:S(2)}) collective-permute-start(f32[2,128,2,128]{3,1,2,0:T(8,128)S(1)} %get-tuple-element.20), channel_id=1, source_target_pairs={{4,0},{8,4},{12,8},{16,12},{20,16},{24,20},{28,24},{32,28},{36,32}... | collective-permute-start | bytes 786440 | tf_op jit(solution)/shard_map/ppermute | solution.py:12
  191.7 18.1 %collective-permute-start.9 = (f32[2,128,2,128]{3,1,2,0:T(8,128)S(1)}, f32[2,128,2,128]{3,1,2,0:T(8,128)S(1)}, u32[]{:S(2)}, u32[]{:S(2)}) collective-permute-start(f32[2,128,2,128]{3,1,2,0:T(8,128)S(1)} %get-tuple-element.21), channel_id=1, source_target_pairs={{8,0},{12,4},{16,8},{20,12},{24,16},{28,20},{32,24},{36,28},{40,32... | collective-permute-start | bytes 786440 | tf_op jit(solution)/shard_map/ppermute | solution.py:12
  194.4 18.9 %collective-permute-start.10 = (f32[2,128,2,128]{3,1,2,0:T(8,128)S(1)}, f32[2,128,2,128]{3,1,2,0:T(8,128)S(1)}, u32[]{:S(2)}, u32[]{:S(2)}) collective-permute-start(f32[2,128,2,128]{3,1,2,0:T(8,128)S(1)} %get-tuple-element.22), channel_id=1, source_target_pairs={{12,0},{16,4},{20,8},{24,12},{28,16},{32,20},{36,24},{40,28},{44,3... | collective-permute-start | bytes 786440 | tf_op jit(solution)/shard_map/ppermute | solution.py:12
  197.5 40.2 %collective-permute-start.11 = (f32[2,128,2,128]{3,1,2,0:T(8,128)}, f32[2,128,2,128]{3,1,2,0:T(8,128)}, u32[]{:S(2)}, u32[]{:S(2)}) collective-permute-start(f32[2,128,2,128]{3,1,2,0:T(8,128)} %get-tuple-element.23), channel_id=1, source_target_pairs={{16,0},{20,4},{24,8},{28,12},{32,16},{36,20},{40,24},{44,28},{48,3... | collective-permute-start | bytes 786440 | tf_op jit(solution)/shard_map/ppermute | solution.py:12
  200.7 42.8 %collective-permute-start.12 = (f32[2,128,2,128]{3,1,2,0:T(8,128)}, f32[2,128,2,128]{3,1,2,0:T(8,128)}, u32[]{:S(2)}, u32[]{:S(2)}) collective-permute-start(f32[2,128,2,128]{3,1,2,0:T(8,128)} %get-tuple-element.24), channel_id=1, source_target_pairs={{20,0},{24,4},{28,8},{32,12},{36,16},{40,20},{44,24},{48,28},{52,3... | collective-permute-start | bytes 786440 | tf_op jit(solution)/shard_map/ppermute | solution.py:12
  204.8 44.3 %collective-permute-start.13 = (f32[2,128,2,128]{3,1,2,0:T(8,128)}, f32[2,128,2,128]{3,1,2,0:T(8,128)}, u32[]{:S(2)}, u32[]{:S(2)}) collective-permute-start(f32[2,128,2,128]{3,1,2,0:T(8,128)} %get-tuple-element.25), channel_id=1, source_target_pairs={{24,0},{28,4},{32,8},{36,12},{40,16},{44,20},{48,24},{52,28},{56,3... | collective-permute-start | bytes 786440 | tf_op jit(solution)/shard_map/ppermute | solution.py:12
  209.8 43.1 %collective-permute-start.15 = (f32[2,128,2,128]{3,1,2,0:T(8,128)}, f32[2,128,2,128]{3,1,2,0:T(8,128)}, u32[]{:S(2)}, u32[]{:S(2)}) collective-permute-start(f32[2,128,2,128]{3,1,2,0:T(8,128)} %get-tuple-element.26), channel_id=1, source_target_pairs={{32,0},{36,4},{40,8},{44,12},{48,16},{52,20},{56,24},{60,28},{64,3... | collective-permute-start | bytes 786440 | tf_op jit(solution)/shard_map/ppermute | solution.py:12
  213.4 2.3 copy-start.6
  213.4 42.2 %collective-permute-start.14 = (f32[2,128,2,128]{3,1,2,0:T(8,128)S(1)}, f32[2,128,2,128]{3,1,2,0:T(8,128)}, u32[]{:S(2)}, u32[]{:S(2)}) collective-permute-start(f32[2,128,2,128]{3,1,2,0:T(8,128)S(1)} %get-tuple-element.27), channel_id=1, source_target_pairs={{28,0},{32,4},{36,8},{40,12},{44,16},{48,20},{52,24},{56,28},{60,3... | collective-permute-start | bytes 786440 | tf_op jit(solution)/shard_map/ppermute | solution.py:12
Sparse Core Ops, SparseCore 0:
  11.6 138.1 all-gather.2
  169.6 33.5 reduce-scatter.2
  205.8 431.9 reduce-scatter.4
